TPU v7x, 128 devices: a whole 4x4x4 slice. The times are simulated.
128 devices in a mesh: ctx: 16 (over x_lo, z, core), tp: 8 (over y, x_hi).
Axes of the slice: x: 4 (x_hi: 2, x_lo: 2; x = x_hi * 2 + x_lo), y: 4, z: 4, core: 2. Of those that a mesh axis runs over, the one named last changes fastest.
Arguments:
- queries: bfloat16 [8192, 4096], P('ctx', 'tp'), may hold values from -6 to 6
- key_rows: bfloat16 [8192, 4096], P('ctx', 'tp'), may hold values from -6 to 6
- value_rows: bfloat16 [8192, 4096], P('ctx', 'tp'), may hold values from -30 to 30
- selection: int32 [16, 3], replicated, may hold values from 0 to 15, as said below
- out_weight: bfloat16 [4096, 7168], P('tp'), may hold values from -0.125 to 0.125
Outputs:
- mixed: bfloat16 [8192, 7168], P('ctx', 'tp')
Inputs may be any that keep to these rules, and one draw needn't show every extreme that they name: Row q of selection lists q first, then 3 - 1 distinct blocks below q; where fewer than that lie below q, the remaining entries are q.
All inputs are finite; a program needn't handle non-finite values.
Results may differ from a plain program's by a relative error of at most 0.013.
Values may be sent and summed in bfloat16 or wider, within the bound.
No kernel may reach another device: no remote copies, remote signals or barrier semaphores. Data moves between devices by JAX's collectives and lax.ppermute only.
A program may use at most 192 MiB of HBM per device.

v0:
```python
import jax
import jax.numpy as jnp
from jax import lax
from jax.sharding import PartitionSpec as P

HD = 128
BLOCK = 512
neg_fill = -1e30


def per_device(queries, key_rows, value_rows, selection, out_weight):
    row_count, feat_width = queries.shape
    head_count = feat_width // HD
    blocks_here = row_count // BLOCK
    block_total = selection.shape[0]
    ctx_place = lax.axis_index("ctx")
    first_row = ctx_place * row_count
    scaling = 1.0 / jnp.sqrt(jnp.float32(HD))
    query_heads = queries.reshape(row_count, head_count, HD).transpose(1, 0, 2)
    own_choice = lax.dynamic_slice_in_dim(selection, ctx_place * blocks_here, blocks_here, 0)
    repeated = jnp.concatenate(
        [jnp.zeros((blocks_here, 1), bool), own_choice[:, 1:] == own_choice[:, :1]], axis=1
    )
    block_ids = jnp.arange(block_total, dtype=jnp.int32)
    chosen = jnp.any(
        (own_choice[:, :, None] == block_ids[None, None, :])
        & jnp.logical_not(repeated)[:, :, None],
        axis=1,
    )
    query_pos = first_row + jnp.arange(row_count, dtype=jnp.int32)
    initial = (
        jnp.full((head_count, row_count), neg_fill, jnp.float32),
        jnp.zeros((head_count, row_count), jnp.float32),
        jnp.zeros((head_count, row_count, HD), jnp.float32),
    )
    key_piece = lax.all_gather(key_rows, "ctx", axis=0, tiled=True)
    value_piece = lax.all_gather(value_rows, "ctx", axis=0, tiled=True)
    piece_rows = key_piece.shape[0]
    key_pos = jnp.arange(piece_rows, dtype=jnp.int32)
    in_block = (key_pos // BLOCK)[None, :] == block_ids[:, None]
    blockwise = jnp.any(chosen[:, :, None] & in_block[None, :, :], axis=1)
    allowed = jnp.broadcast_to(blockwise[:, None, :], (blocks_here, BLOCK, piece_rows)).reshape(
        row_count, piece_rows
    )
    allowed = allowed & (key_pos[None, :] <= query_pos[:, None])

    def compute(state):
        run_max, run_sum, run_acc = state
        key_heads = key_piece.reshape(piece_rows, head_count, HD).transpose(1, 0, 2)
        value_heads = value_piece.reshape(piece_rows, head_count, HD).transpose(1, 0, 2)
        scores = (
            jnp.einsum("htd,hsd->hts", query_heads, key_heads, preferred_element_type=jnp.float32)
            * scaling
        )
        new_max = jnp.maximum(run_max, jnp.max(jnp.where(allowed[None], scores, neg_fill), axis=-1))
        expo = jnp.where(allowed[None], jnp.exp(scores - new_max[..., None]), 0.0)
        new_sum = jnp.sum(expo, axis=-1)
        weights = expo.astype(jnp.bfloat16)
        new_acc = jnp.einsum(
            "hts,hsd->htd", weights, value_heads, preferred_element_type=jnp.float32
        )
        return (new_max, new_sum, new_acc)

    run_max, run_sum, run_acc = lax.cond(jnp.any(allowed), compute, lambda state: state, initial)
    attended = (
        (run_acc / run_sum[..., None])
        .astype(jnp.bfloat16)
        .transpose(1, 0, 2)
        .reshape(row_count, feat_width)
    )
    shares = lax.psum_scatter(
        lax.dot_general(
            out_weight, attended, (((0,), (1,)), ((), ())), preferred_element_type=jnp.float32
        ).astype(jnp.bfloat16),
        "tp",
        scatter_dimension=0,
        tiled=True,
    ).astype(jnp.float32)
    mixed_out = jnp.transpose(shares)
    return mixed_out.astype(jnp.bfloat16)


def solution(mesh):
    placed = (P("ctx", "tp"), P("ctx", "tp"), P("ctx", "tp"), P(), P("tp", None))
    return jax.shard_map(
        per_device, mesh=mesh, in_specs=placed, out_specs=P("ctx", "tp"), check_vma=False
    )
```

profile of v0, /device:TPU:1, one launch (start us, length us, event | category | flops | bytes accessed | tf_op | source)
XLA Modules:
  0.0 339.7 jit_solution(13768091969145868570)
XLA Ops:
  6.5 0.0 all-gather.3.cloned.1.call-start
  6.5 0.7 all-gather.3.cloned.1.call-update
  7.3 0.0 all-gather.5.cloned.1.call-start
  7.3 0.7 all-gather.5.cloned.1.call-update
  8.0 0.0 reduce-scatter.4.cloned.1.call-start
  8.1 0.9 fusion.20
  8.9 0.5 slice.7
  9.4 1.3 copy.20
  10.7 0.8 compare_reduce_fusion
  11.5 0.1 add_not_fusion
  11.6 0.1 fusion.18
  11.6 0.2 fusion.13
  11.8 7.3 %fusion.10 = (pred[512,8192]{1,0:T(8,128)(4,1)}, pred[]{:T(512)}) fusion(s32[512]{0:T(512)S(1)} %iota_add_fusion, pred[8192]{0:T(1024)(128)(4,1)S(1)} %fusion.13), kind=kLoop, calls=%fused_computation.15 | loop fusion | flops 12582911 | bytes 4204545 | tf_op jit(solution)/shard_map/and | solution.py:45
  19.8 45.1 %all-gather.3.cloned.1.call-done = bf16[8192,512]{1,0:T(8,128)(2,1)} async-done(((bf16[512,512]{1,0:T(8,128)(2,1)}), bf16[8192,512]{1,0:T(8,128)(2,1)}) %all-gather.3.cloned.1.call-update) | async-done | bytes 8388624 | tf_op jit(solution)/shard_map/all_gather | solution.py:36
  64.9 54.9 %all-gather.5.cloned.1.call-done = bf16[8192,512]{1,0:T(8,128)(2,1)} async-done(((bf16[512,512]{1,0:T(8,128)(2,1)}), bf16[8192,512]{1,0:T(8,128)(2,1)}) %all-gather.5.cloned.1.call-update) | async-done | bytes 8388624 | tf_op jit(solution)/shard_map/all_gather | solution.py:37
  119.8 84.5 %conditional.1 = (f32[4,512]{1,0:T(4,128)S(1)}, f32[4,512,128]{1,2,0:T(8,128)S(1)}) conditional(s32[]{:T(128)} %convert_element_type.20, () %tuple.13, (pred[512,8192]{1,0:T(8,128)(4,1)}, bf16[8192,512]{1,0:T(8,128)(2,1)}, bf16[4,512,128]{1,2,0:T(8,128)(2,1)S(1)}, bf16[8192,512]{1,0:T(8,128)(2,1)}) %tuple.31), branch_computations={%region_3.4_spmd, %region_4.7_spmd} | conditional | flops 8774481920 | bytes 232308752 | solution.py:64
  119.8 29.7 %select_reduce_fusion = (f32[4,512]{1,0:T(4,128)S(1)}, f32[4,512,8192]{2,1,0:T(8,128)}) fusion(pred[512,8192]{1,0:T(8,128)(4,1)} %get-tuple-element.13, bf16[4,512,128]{1,2,0:T(8,128)(2,1)S(1)} %get-tuple-element.31, bf16[8192,512]{1,0:T(8,128)(2,1)} %get-tuple-element.15), kind=kOutput, calls=%fused_computation.1 | convolution fusion | flops 4345296896 | bytes 80224256 | tf_op jit(solution)/shard_map/cond/branch_1_fun/htd,hsd->hts/dot_general | solution.py:52
  149.5 31.8 %fusion.2 = f32[4,512,128]{1,2,0:T(8,128)S(1)} fusion(f32[4,512,8192]{2,1,0:T(8,128)} %get-tuple-element.37, f32[4,512]{1,0:T(4,128)S(1)} %broadcast_maximum_fusion, pred[512,8192]{1,0:T(8,128)(4,1)} %get-tuple-element.13, bf16[8192,512]{1,0:T(8,128)(2,1)} %get-tuple-element.16), kind=kOutput, calls=%fused_computation.4 | convolution fusion | flops 4362076160 | bytes 80748544 | tf_op jit(solution)/shard_map/cond | solution.py:64
  181.3 22.7 %fusion.1 = f32[4,512]{1,0:T(4,128)S(1)} fusion(f32[4,512,8192]{2,1,0:T(8,128)} %get-tuple-element.37, f32[4,512]{1,0:T(4,128)S(1)} %broadcast_maximum_fusion, pred[512,8192]{1,0:T(8,128)(4,1)} %get-tuple-element.13), kind=kLoop, calls=%fused_computation.3 | loop fusion | flops 67106816 | bytes 71319552 | tf_op jit(solution)/shard_map/cond/branch_1_fun/reduce_sum | solution.py:57
  204.2 0.1 divide_convert_fusion
  204.4 9.2 %fusion.11 = bf16[7168,512]{0,1:T(8,128)(2,1)} fusion(bf16[512,512]{0,1:T(8,128)(2,1)S(1)} %bitcast.38, bf16[512,7168]{1,0:T(8,128)(2,1)} %param.11), kind=kOutput, calls=%fused_computation.17 | convolution fusion | flops 3761766400 | bytes 15204352 | tf_op jit(solution)/shard_map/dot_general | solution.py:72
  213.6 10.4 %copy.24 = bf16[7168,512]{1,0:T(8,128)(2,1)} copy(bf16[7168,512]{0,1:T(8,128)(2,1)} %fusion.11) | data formatting | bytes 14680064
  224.0 0.0 reduce-scatter.4.cloned.1.call-update
  224.0 106.9 %reduce-scatter.4.cloned.1.call-done = bf16[896,512]{1,0:T(8,128)(2,1)} async-done(((bf16[7168,512]{1,0:T(8,128)(2,1)}), bf16[896,512]{1,0:T(8,128)(2,1)}) %reduce-scatter.4.cloned.1.call-update) | async-done | bytes 917520
  330.9 2.2 copy.25
  (3 shorter events, 0.0 us)
Async XLA Ops:
  6.5 58.4 %all-gather.3.cloned.1.call-start = ((), (), s32[]{:S(2)}) async-start(), calls=%async_computation.1 | async-start | bytes 8912896 | tf_op jit(solution)/shard_map/all_gather | solution.py:36
  7.3 112.5 %all-gather.5.cloned.1.call-start = ((), (), s32[]{:S(2)}) async-start(), calls=%async_computation.2 | async-start | bytes 8912896 | tf_op jit(solution)/shard_map/all_gather | solution.py:37
  8.0 322.9 %reduce-scatter.4.cloned.1.call-start = ((), (), s32[]{:S(2)}) async-start(), calls=%async_computation.3 | async-start | bytes 8257536
Sparse Core Ops, SparseCore 0:
  9.1 55.7 all-gather.2
  66.6 53.1 all-gather.4
  224.2 106.7 reduce-scatter.3
where the time goes:
time: 340 us
  waiting for transfers between devices  208 us (61%)
  matrix products  70.8 us (21%)
  other arithmetic  31.3 us (9%)
  local copies, waits for them, and re-layouts  15.3 us (4%)
  between operations  13.8 us (4%)
    unnamed x4, waiting for transfers between devices  108 us
    all_gather x1, waiting for transfers between devices, per_device(): value_piece = lax.all_gather(value_rows, 'ctx', axis=0, tiled=True)  54.9 us
    all_gather x1, waiting for transfers between devices, per_device(): key_piece = lax.all_gather(key_rows, 'ctx', axis=0, tiled=True)  45.1 us
    cond x1, matrix products, per_device(): lax.cond(jnp.any(allowed), compute, lambda state: state, initial)  31.8 us
    dot_general x1, matrix products, compute(): jnp.einsum('htd,hsd->hts', query_heads, key_heads, preferred_element_type...  29.7 us
    reduce_sum x1, other arithmetic, compute(): new_sum = jnp.sum(expo, axis=-1)  22.7 us
    unnamed x3, local copies, waits for them, and re-layouts  13.9 us
    dot_general x1, matrix products, per_device(): lax.dot_general(out_weight, attended, (((0,), (1,)), ((), ())), preferred...  9.24 us
  transfers between devices with their start and end apart: 3, of which 3 were waited for; matrix products, arithmetic and copies ran while one was open for 3% of the time, Pallas kernels for 0%

commit v1 on v0

--- a/solution.py
+++ b/solution.py
@@ -34,7 +34,9 @@
         jnp.zeros((head_count, row_count, HD), jnp.float32),
     )
     key_piece = lax.all_gather(key_rows, "ctx", axis=0, tiled=True)
-    value_piece = lax.all_gather(value_rows, "ctx", axis=0, tiled=True)
+    value_piece = jnp.concatenate(
+        lax.all_to_all(jnp.stack([value_rows] * lax.axis_size("ctx")), "ctx", 0, 0), axis=0
+    )
     piece_rows = key_piece.shape[0]
     key_pos = jnp.arange(piece_rows, dtype=jnp.int32)
     in_block = (key_pos // BLOCK)[None, :] == block_ids[:, None]

time: 340 us -> 404 us (1.19)
  waiting for transfers between devices: 208 us -> 246 us
  local copies, waits for them, and re-layouts: 15.3 us -> 31.1 us
  starting transfers between devices: 0.08 us -> 7.8 us
    all_to_all x0 -> x1, waiting for transfers between devices: none -> 137 us  [per_device(): lax.all_to_all(jnp.stack([value_rows] * lax.axis_size('ctx')), 'ctx', 0, 0)]
    all_gather x1 -> x0, waiting for transfers between devices: 54.9 us -> none  [per_device(): value_piece = lax.all_gather(value_rows, 'ctx', axis=0, tiled=True)]
    all_gather x1, waiting for transfers between devices: 45.1 us -> 0.01 us  [per_device(): key_piece = lax.all_gather(key_rows, 'ctx', axis=0, tiled=True)]
    another operation x0 -> x2, local copies, waits for them, and re-layouts: none -> 17.6 us  [the longest x1 12.5 us: compute(): value_piece.reshape(piece_rows, head_count, HD).transpose(1, 0, 2)]
    all_to_all x0 -> x1, starting transfers between devices: none -> 7.76 us  [per_device(): lax.all_to_all(jnp.stack([value_rows] * lax.axis_size('ctx')), 'ctx', 0, 0)]
    unnamed x3 -> x7, local copies, waits for them, and re-layouts: 13.9 us -> 12.8 us
    unnamed x4 -> x3, waiting for transfers between devices: 108 us -> 109 us
  transfers between devices with their start and end apart: 3 -> 3, of which waited for: 3 -> 2; matrix products, arithmetic and copies ran while one was open for 3% -> 4% of each run, Pallas kernels for 0% -> 0%
where the time goes in v1:
time: 404 us; the launch traced here: 403 us
  waiting for transfers between devices  246 us (61%)
  matrix products  72.1 us (18%)
  other arithmetic  31.4 us (8%)
  local copies, waits for them, and re-layouts  31.1 us (8%)
  between operations  14.1 us (3%)
  starting transfers between devices  7.8 us (2%)
    all_to_all x1, waiting for transfers between devices, per_device(): lax.all_to_all(jnp.stack([value_rows] * lax.axis_size('ctx')), 'ctx', 0, 0)  137 us
    unnamed x3, waiting for transfers between devices  109 us
    cond x1, matrix products, per_device(): lax.cond(jnp.any(allowed), compute, lambda state: state, initial)  33.2 us
    dot_general x1, matrix products, compute(): jnp.einsum('htd,hsd->hts', query_heads, key_heads, preferred_element_type...  29.7 us
    reduce_sum x1, other arithmetic, compute(): new_sum = jnp.sum(expo, axis=-1)  22.9 us
    unnamed x7, local copies, waits for them, and re-layouts  12.8 us
    another operation x1, local copies, waits for them, and re-layouts, compute(): value_piece.reshape(piece_rows, head_count, HD).transpose(1, 0, 2)  12.5 us
    dot_general x1, matrix products, per_device(): lax.dot_general(out_weight, attended, (((0,), (1,)), ((), ())), preferred...  9.24 us
  transfers between devices with their start and end apart: 3, of which 2 were waited for; matrix products, arithmetic and copies ran while one was open for 4% of the time, Pallas kernels for 0%

profile of v1, /device:TPU:1, one launch (start us, length us, event | category | flops | bytes accessed | tf_op | source)
XLA Modules:
  0.0 402.7 jit_solution(17212824046103471834)
XLA Ops:
  6.5 0.0 copy-start.1
  6.5 0.0 copy-start
  6.5 0.0 all-gather.2.cloned.1.call-start
  6.5 0.7 all-gather.2.cloned.1.call-update
  7.3 5.1 %stack.2 = bf16[16,512,512]{2,1,0:T(8,128)(2,1)} broadcast(bf16[512,512]{1,0:T(8,128)(2,1)} %param.9), dimensions={1,2} | broadcast | bytes 8912896 | tf_op jit(solution)/shard_map/stack | solution.py:38
  12.3 7.8 %all-to-all-start = ((bf16[16,512,512]{2,1,0:T(8,128)(2,1)}), bf16[16,512,512]{2,1,0:T(8,128)(2,1)}, u32[]{:S(2)}, u32[]{:S(2)}) async-start(bf16[16,512,512]{2,1,0:T(8,128)(2,1)} %stack.2), calls=%async_computation | async-start | bytes 16777216 | tf_op jit(solution)/shard_map/all_to_all | solution.py:38
  20.1 0.0 reduce-scatter.4.cloned.1.call-start
  20.1 0.0 copy-done.1
  20.2 0.2 fusion.21
  20.3 0.5 slice.7
  20.9 0.0 copy-done
  20.9 0.2 copy.20
  21.1 0.8 compare_reduce_fusion
  21.9 0.1 add_not_fusion
  21.9 0.1 fusion.19
  22.0 0.2 fusion.14
  22.2 7.3 %fusion.11 = (pred[512,8192]{1,0:T(8,128)(4,1)}, pred[]{:T(512)}) fusion(s32[512]{0:T(512)S(1)} %iota_add_fusion, pred[8192]{0:T(1024)(128)(4,1)S(1)} %fusion.14), kind=kLoop, calls=%fused_computation.15 | loop fusion | flops 12582911 | bytes 4204545 | tf_op jit(solution)/shard_map/and | solution.py:47
  30.2 136.7 %all-to-all-done = bf16[16,512,512]{2,1,0:T(8,128)(2,1)} async-done(((bf16[16,512,512]{2,1,0:T(8,128)(2,1)}), bf16[16,512,512]{2,1,0:T(8,128)(2,1)}, u32[]{:S(2)}, u32[]{:S(2)}) %all-to-all-start) | async-done | bytes 8388640 | tf_op jit(solution)/shard_map/all_to_all | solution.py:38
  166.9 0.0 all-gather.2.cloned.1.call-done
  166.9 98.4 %conditional.1 = (f32[4,512]{1,0:T(4,128)S(1)}, f32[4,512,128]{1,2,0:T(8,128)S(1)}) conditional(s32[]{:T(128)} %convert_element_type.20, () %tuple.13, (pred[512,8192]{1,0:T(8,128)(4,1)}, bf16[8192,512]{1,0:T(8,128)(2,1)}, bf16[4,512,128]{1,2,0:T(8,128)(2,1)S(1)}, bf16[16,512,512]{2,1,0:T(8,128)(2,1)}) %tuple.29), branch_computations={%region_3.4_spmd, %region_4.7_spmd} | conditional | flops 8774481920 | bytes 249085968 | solution.py:66
  166.9 12.5 %reshape_reshape.2 = bf16[8192,4,128]{2,1,0:T(4,128)(2,1)} reshape(bf16[16,512,512]{2,1,0:T(8,128)(2,1)} %get-tuple-element.16) | data formatting | bytes 16777216 | tf_op jit(solution)/shard_map/cond/branch_1_fun/reshape;reshape | solution.py:52
  179.4 29.7 %select_reduce_fusion = (f32[4,512]{1,0:T(4,128)S(1)}, f32[4,512,8192]{2,1,0:T(8,128)}) fusion(pred[512,8192]{1,0:T(8,128)(4,1)} %get-tuple-element.13, bf16[4,512,128]{1,2,0:T(8,128)(2,1)S(1)} %get-tuple-element.31, bf16[8192,512]{1,0:T(8,128)(2,1)} %get-tuple-element.15), kind=kOutput, calls=%fused_computation.1 | convolution fusion | flops 4345296896 | bytes 80224256 | tf_op jit(solution)/shard_map/cond/branch_1_fun/htd,hsd->hts/dot_general | solution.py:54
  209.1 33.2 %fusion.2 = f32[4,512,128]{1,2,0:T(8,128)S(1)} fusion(f32[4,512,8192]{2,1,0:T(8,128)} %get-tuple-element.37, f32[4,512]{1,0:T(4,128)S(1)} %broadcast_maximum_fusion, pred[512,8192]{1,0:T(8,128)(4,1)} %get-tuple-element.13, bf16[8192,4,128]{2,1,0:T(4,128)(2,1)} %reshape_reshape.2), kind=kOutput, calls=%fused_computation.4 | convolution fusion | flops 4362076160 | bytes 80748544 | tf_op jit(solution)/shard_map/cond | solution.py:66
  242.3 22.9 %fusion.1 = f32[4,512]{1,0:T(4,128)S(1)} fusion(f32[4,512,8192]{2,1,0:T(8,128)} %get-tuple-element.37, f32[4,512]{1,0:T(4,128)S(1)} %broadcast_maximum_fusion, pred[512,8192]{1,0:T(8,128)(4,1)} %get-tuple-element.13), kind=kLoop, calls=%fused_computation.3 | loop fusion | flops 67106816 | bytes 71319552 | tf_op jit(solution)/shard_map/cond/branch_1_fun/reduce_sum | solution.py:59
  265.3 0.1 divide_convert_fusion
  265.5 9.2 %fusion.12 = bf16[7168,512]{0,1:T(8,128)(2,1)} fusion(bf16[512,512]{0,1:T(8,128)(2,1)S(1)} %bitcast.31, bf16[512,7168]{1,0:T(8,128)(2,1)} %param.11), kind=kOutput, calls=%fused_computation.17 | convolution fusion | flops 3761766400 | bytes 15204352 | tf_op jit(solution)/shard_map/dot_general | solution.py:74
  274.7 10.4 %copy.24 = bf16[7168,512]{1,0:T(8,128)(2,1)} copy(bf16[7168,512]{0,1:T(8,128)(2,1)} %fusion.12) | data formatting | bytes 14680064
  285.1 0.0 reduce-scatter.4.cloned.1.call-update
  285.1 108.6 %reduce-scatter.4.cloned.1.call-done = bf16[896,512]{1,0:T(8,128)(2,1)} async-done(((bf16[7168,512]{1,0:T(8,128)(2,1)}), bf16[896,512]{1,0:T(8,128)(2,1)}) %reduce-scatter.4.cloned.1.call-update) | async-done | bytes 917520
  393.7 2.2 copy.25
  (3 shorter events, 0.0 us)
Async XLA Ops:
  6.5 13.6 %copy-start.1 = (s32[16,3]{0,1:T(4,128)S(1)}, s32[16,3]{0,1:T(4,128)}, u32[]{:S(2)}) copy-start(s32[16,3]{0,1:T(4,128)} %param.10) | copy-start | bytes 580
  6.5 14.3 %copy-start = (bf16[512,512]{1,0:T(8,128)(2,1)S(1)}, bf16[512,512]{1,0:T(8,128)(2,1)}, u32[]{:S(2)}) copy-start(bf16[512,512]{1,0:T(8,128)(2,1)} %param.7) | copy-start | bytes 1572868
  6.5 160.3 %all-gather.2.cloned.1.call-start = ((), (), s32[]{:S(2)}) async-start(), calls=%async_computation.2 | async-start | bytes 8912896 | tf_op jit(solution)/shard_map/all_gather | solution.py:36
  12.3 154.5 %all-to-all-start = ((bf16[16,512,512]{2,1,0:T(8,128)(2,1)}), bf16[16,512,512]{2,1,0:T(8,128)(2,1)}, u32[]{:S(2)}, u32[]{:S(2)}) async-start(bf16[16,512,512]{2,1,0:T(8,128)(2,1)} %stack.2), calls=%async_computation | async-start | bytes 16777216 | tf_op jit(solution)/shard_map/all_to_all | solution.py:38
  20.1 373.6 %reduce-scatter.4.cloned.1.call-start = ((), (), s32[]{:S(2)}) async-start(), calls=%async_computation.3 | async-start | bytes 8257536
Sparse Core Ops, SparseCore 0:
  9.1 147.3 all-gather.1
  285.3 108.3 reduce-scatter.3
